TPU v7x, 32 devices: a whole 2x2x4 slice. The times are simulated.
32 devices in a mesh: case: 2 (over y), tm: 4 (over z), bundle: 2 (over x), sub: 2 (over core).
Axes of the slice: x: 2, y: 2, z: 4, core: 2. Of those that a mesh axis runs over, the one named last changes fastest.
Arguments:
- cotangent: bfloat16 [16384, 512], P(('case', 'tm'), 'bundle'), parts along dimension 0, may hold values from -28 to 28
- inputs: bfloat16 [16384, 512], P(('case', 'tm'), 'bundle'), parts along dimension 0, may hold values from -6 to 6
- impulse: bfloat16 [8, 128, 4096], P('bundle', 'sub'), may hold values from -0.0625 to 0.0625
- terminal: int32 [8, 64], P('bundle'), may hold values from 0 to 63, each once within a row
- fault_step: int32 [2], P('case'), parts along dimension 0, may hold values from 0 to 4095
Outputs:
- voltage_grad: bfloat16 [16384, 512], P(('case', 'tm', 'sub'), 'bundle'), parts along dimension 0
- impulse_grad: float32 [16, 128, 4096], P(('case', 'bundle'), 'sub', 'tm'), parts along dimension 0
There are 2 independent parts, one for each index of `case`. A program takes and returns all parts, laid end to end along the dimension named above; an argument that names none is the same for every part. Nothing has to cross between parts.
Inputs may be any that keep to these rules, and one draw needn't show every extreme that they name: Each row of terminal orders the 64 terminals of a bundle, each once.
All inputs are finite; a program needn't handle non-finite values.
Results may differ from a plain program's by a relative error of at most 0.001.
Values may be sent and summed in bfloat16 or wider, within the bound.
No kernel may reach another device: no remote copies, remote signals or barrier semaphores. Data moves between devices by JAX's collectives and lax.ppermute only.
A program may use at most 320 MiB of HBM per device.

v0:
```python
import math
import jax
import jax.numpy as jnp
from jax import lax
from jax.sharding import PartitionSpec as P

CB = 64
NB = 8
L = 128
norm_ratio = 0.5
tile_rows = 8


def passed_along(block, axis, distance):
    devices = range(lax.axis_size(axis))
    route = [(i - distance, i) for i in devices if i - distance in devices]
    return lax.ppermute(block, axis, route)


def tiles_of(source, start, block_rows, lag_count):
    bundles = source.shape[0]
    width = source.shape[2]
    window = lax.dynamic_slice_in_dim(source, start, block_rows + lag_count, 1)
    tiled = window.reshape(bundles, (block_rows + lag_count) // tile_rows, tile_rows, width)
    tile_count = block_rows // tile_rows
    spans = [tiled[:, first : first + tile_count] for first in range(lag_count // tile_rows + 1)]
    wide = jnp.concatenate(spans, axis=2)
    return wide.reshape(bundles, tile_count, (lag_count + tile_rows) * width)


def local(cotangent, inputs, impulse, terminal, fault_step):
    seg_rows = cotangent.shape[0]
    local_bundles = terminal.shape[0]
    bundle_width = terminal.shape[1]
    lag_count = impulse.shape[1]
    all_lags = lag_count * lax.axis_size("sub")
    lag_first = lax.axis_index("sub") * lag_count
    columns = jnp.arange(bundle_width, dtype=jnp.int32)
    onehot = (terminal[:, :, None] == columns[None, None, :]).astype(jnp.bfloat16)
    grad_in = cotangent.reshape(seg_rows, local_bundles, bundle_width)
    reordered = jnp.einsum(
        "tbi,bir->tbr", grad_in, onehot, preferred_element_type=jnp.float32
    ).astype(jnp.bfloat16)
    seg_start = lax.axis_index("tm") * seg_rows
    steps_here = seg_start + jnp.arange(seg_rows, dtype=jnp.int32)
    live_rows = steps_here >= fault_step[0]
    masked = jnp.where(
        live_rows[:, None, None],
        inputs.reshape(seg_rows, local_bundles, bundle_width),
        jnp.zeros((), jnp.bfloat16),
    )
    ahead_rows = passed_along(reordered[:all_lags], "tm", -1)
    extended = jnp.concatenate([reordered, ahead_rows], axis=0)
    ext_lanes = jnp.transpose(extended, (1, 0, 2))
    reord_lanes = jnp.transpose(reordered, (1, 0, 2))
    kernel = impulse.reshape(local_bundles, lag_count, bundle_width, bundle_width)
    zero_pad = jnp.zeros((local_bundles, tile_rows, bundle_width, bundle_width), jnp.bfloat16)
    kernel_pad = jnp.concatenate([zero_pad, kernel, zero_pad], axis=1)
    toeplitz = jnp.stack(
        [
            kernel_pad[:, tile_rows - shift_row : tile_rows - shift_row + lag_count + tile_rows]
            for shift_row in range(tile_rows)
        ],
        axis=3,
    )
    toeplitz = toeplitz.reshape(
        local_bundles, (lag_count + tile_rows) * bundle_width, tile_rows * bundle_width
    )
    block_rows = min(512, seg_rows)
    block_count = seg_rows // block_rows
    tile_count = block_rows // tile_rows
    behind = passed_along(masked[seg_rows - all_lags :], "tm", 1)
    history = jnp.concatenate([behind, masked], axis=0)
    hist_lanes = jnp.transpose(history, (1, 0, 2))

    def advance(grad_acc, block_index):
        row_start = block_index * block_rows
        wide = tiles_of(ext_lanes, row_start + lag_first, block_rows, lag_count)
        dx_block = jnp.einsum("bkx,bxy->bky", wide, toeplitz, preferred_element_type=jnp.float32)
        row_block = lax.dynamic_slice_in_dim(reord_lanes, row_start, block_rows, 1).reshape(
            local_bundles, tile_count, tile_rows * bundle_width
        )
        earlier = tiles_of(
            hist_lanes, row_start + all_lags - lag_first - lag_count, block_rows, lag_count
        )
        grad_acc = grad_acc + jnp.einsum(
            "bkx,bky->bxy", row_block, earlier, preferred_element_type=jnp.float32
        )
        return (grad_acc, dx_block.reshape(local_bundles, block_rows, bundle_width))

    acc_shape = (local_bundles, tile_rows * bundle_width, (lag_count + tile_rows) * bundle_width)
    grad_total, dx_blocks = lax.scan(
        advance, jnp.zeros(acc_shape, jnp.float32), jnp.arange(block_count, dtype=jnp.int32)
    )
    partial_dx = jnp.transpose(dx_blocks, (0, 2, 1, 3)).reshape(
        seg_rows, local_bundles * bundle_width
    )
    folded = grad_total.reshape(
        local_bundles, tile_rows, bundle_width, lag_count + tile_rows, bundle_width
    )
    lag_sum = folded[:, 0, :, 1 : lag_count + 1, :]
    for shift_row in range(1, tile_rows):
        lag_sum = lag_sum + folded[:, shift_row, :, shift_row + 1 : shift_row + lag_count + 1, :]
    grad_blocks = jnp.transpose(jnp.flip(lag_sum, axis=2), (0, 2, 1, 3))
    summed_dx = lax.psum_scatter(partial_dx, "sub", scatter_dimension=0, tiled=True)
    share_rows = summed_dx.shape[0]
    own_steps = (
        seg_start + lax.axis_index("sub") * share_rows + jnp.arange(share_rows, dtype=jnp.int32)
    )
    voltage_grad = jnp.where((own_steps >= fault_step[0])[:, None], summed_dx, 0.0).astype(
        jnp.bfloat16
    )
    grad_flat = grad_blocks.reshape(local_bundles, lag_count, bundle_width * bundle_width)
    grad_sum = lax.psum(grad_flat, "tm")
    share_cols = grad_flat.shape[2] // lax.axis_size("tm")
    own_grad = lax.dynamic_slice_in_dim(grad_sum, lax.axis_index("tm") * share_cols, share_cols, 2)
    own_squares = jnp.sum(own_grad * own_grad)
    total_squares = lax.psum(own_squares, ("tm", "bundle", "sub"))
    norm_limit = norm_ratio * math.sqrt(NB * L * CB * CB)
    factor = norm_limit / jnp.sqrt(total_squares + 1e-06)
    return (voltage_grad, own_grad * factor)


def solution(mesh):
    placed = (
        P(("case", "tm"), "bundle"),
        P(("case", "tm"), "bundle"),
        P("bundle", "sub", None),
        P("bundle", None),
        P("case"),
    )
    return jax.shard_map(
        local,
        mesh=mesh,
        in_specs=placed,
        out_specs=(P(("case", "tm", "sub"), "bundle"), P(("case", "bundle"), "sub", "tm")),
        check_vma=False,
    )
```

profile of v0, /device:TPU:0, one launch (start us, length us, event | category | flops | bytes accessed | tf_op | source)
XLA Modules:
  0.0 749.6 jit_solution(2607385197991196513)
XLA Ops:
  8.1 1.6 copy.41
  9.6 2.1 convolution_convert_fusion
  15.3 5.6 collective-permute-start
  20.9 4.8 copy.43
  25.6 6.1 bitcast_dynamic-update-slice_fusion
  32.8 4.1 pad_maximum_fusion
  36.9 3.3 fusion.7
  40.2 3.2 fusion.6
  43.4 3.2 fusion.5
  46.6 3.2 fusion.4
  49.9 3.2 fusion.3
  53.1 3.3 fusion.2
  56.4 3.4 fusion.1
  59.8 47.4 %copy.50 = bf16[4,72,64,8,64]{4,3,2,1,0:T(8,128)(2,1)} copy(bf16[4,72,64,8,64]{1,4,3,2,0:T(8,128)(2,1)} %fusion.1) | data formatting | bytes 37748736 | tf_op jit(solution)/shard_map/stack | solution.py:59
  107.2 49.1 %reshape.92 = bf16[4,4608,512]{2,1,0:T(8,128)(2,1)} reshape(bf16[4,72,64,8,64]{4,3,2,1,0:T(8,128)(2,1)} %copy.50) | data formatting | bytes 37748736 | tf_op jit(solution)/shard_map/reshape | solution.py:66
  156.3 2.3 maximum_bitcast_fusion.1
  159.7 269.9 %while.17 = (s32[]{:T(128)}, f32[4,512,4608]{2,1,0:T(8,128)}, f32[4,4,512,64]{3,2,1,0:T(8,128)}, s32[4]{0:T(128)S(1)}, bf16[4,2048,64]{1,2,0:T(8,128)(2,1)}, /*i...) while((s32[]{:T(128)}, f32[4,512,4608]{2,1,0:T(8,128)}, ...), condition=%wide.region_1.2_spmd.clone, body=%wide.region_0.1_spmd.clone.sunk | while | flops 2434793472 | bytes 131072384 | solution.py:92
  163.2 1.5 constant_dynamic-slice_fusion.6
  173.4 6.1 reshape.109
  179.5 8.1 %fusion.24 = f32[4,64,512]{2,1,0:T(8,128)S(1)} fusion(bf16[4,64,4608]{2,1,0:T(8,128)(2,1)S(1)} %reshape.109, bf16[4,4608,512]{2,1,0:T(8,128)(2,1)} %get-tuple-element.366), kind=kOutput, calls=%fused_computation.58.clone.1 | convolution fusion | flops 1207959552 | bytes 21757952 | tf_op jit(solution)/shard_map/while/body/eval_jaxpr/bkx,bxy->bky/dot_general | solution.py:79
  196.9 6.1 reshape.108
  203.1 14.0 %select_add_fusion.2 = f32[4,512,4608]{2,1,0:T(8,128)} fusion(f32[4,512,4608]{2,1,0:T(8,128)} %get-tuple-element.342, pred[]{:T(512)S(6)} %compare.4, bf16[4,64,512]{2,1,0:T(8,128)(2,1)S(1)} %copy-done.1, bf16[4,64,4608]{2,1,0:T(8,128)(2,1)S(1)} %reshape.108), kind=kOutput, calls=%fused_computation.clone.1 | convolution fusion | flops 1226833920 | bytes 78118912 | tf_op jit(solution)/shard_map/while/body/eval_jaxpr/bkx,bky->bxy/dot_general | solution.py:86
  220.6 1.5 constant_dynamic-slice_fusion.6
  230.8 6.1 reshape.109
  236.9 8.1 %fusion.24 = f32[4,64,512]{2,1,0:T(8,128)S(1)} fusion(bf16[4,64,4608]{2,1,0:T(8,128)(2,1)S(1)} %reshape.109, bf16[4,4608,512]{2,1,0:T(8,128)(2,1)} %get-tuple-element.366), kind=kOutput, calls=%fused_computation.58.clone.1 | convolution fusion | flops 1207959552 | bytes 21757952 | tf_op jit(solution)/shard_map/while/body/eval_jaxpr/bkx,bxy->bky/dot_general | solution.py:79
  254.4 6.1 reshape.108
  260.5 27.4 %select_add_fusion.2 = f32[4,512,4608]{2,1,0:T(8,128)} fusion(f32[4,512,4608]{2,1,0:T(8,128)} %get-tuple-element.342, pred[]{:T(512)S(6)} %compare.4, bf16[4,64,512]{2,1,0:T(8,128)(2,1)S(1)} %copy-done.1, bf16[4,64,4608]{2,1,0:T(8,128)(2,1)S(1)} %reshape.108), kind=kOutput, calls=%fused_computation.clone.1 | convolution fusion | flops 1226833920 | bytes 78118912 | tf_op jit(solution)/shard_map/while/body/eval_jaxpr/bkx,bky->bxy/dot_general | solution.py:86
  291.5 1.5 constant_dynamic-slice_fusion.6
  301.6 6.1 reshape.109
  307.8 8.1 %fusion.24 = f32[4,64,512]{2,1,0:T(8,128)S(1)} fusion(bf16[4,64,4608]{2,1,0:T(8,128)(2,1)S(1)} %reshape.109, bf16[4,4608,512]{2,1,0:T(8,128)(2,1)} %get-tuple-element.366), kind=kOutput, calls=%fused_computation.58.clone.1 | convolution fusion | flops 1207959552 | bytes 21757952 | tf_op jit(solution)/shard_map/while/body/eval_jaxpr/bkx,bxy->bky/dot_general | solution.py:79
  325.2 6.1 reshape.108
  331.4 27.4 %select_add_fusion.2 = f32[4,512,4608]{2,1,0:T(8,128)} fusion(f32[4,512,4608]{2,1,0:T(8,128)} %get-tuple-element.342, pred[]{:T(512)S(6)} %compare.4, bf16[4,64,512]{2,1,0:T(8,128)(2,1)S(1)} %copy-done.1, bf16[4,64,4608]{2,1,0:T(8,128)(2,1)S(1)} %reshape.108), kind=kOutput, calls=%fused_computation.clone.1 | convolution fusion | flops 1226833920 | bytes 78118912 | tf_op jit(solution)/shard_map/while/body/eval_jaxpr/bkx,bky->bxy/dot_general | solution.py:86
  362.3 1.4 constant_dynamic-slice_fusion.6
  372.4 6.1 reshape.109
  378.6 8.1 %fusion.24 = f32[4,64,512]{2,1,0:T(8,128)S(1)} fusion(bf16[4,64,4608]{2,1,0:T(8,128)(2,1)S(1)} %reshape.109, bf16[4,4608,512]{2,1,0:T(8,128)(2,1)} %get-tuple-element.366), kind=kOutput, calls=%fused_computation.58.clone.1 | convolution fusion | flops 1207959552 | bytes 21757952 | tf_op jit(solution)/shard_map/while/body/eval_jaxpr/bkx,bxy->bky/dot_general | solution.py:79
  396.0 6.1 reshape.108
  402.2 27.4 %select_add_fusion.2 = f32[4,512,4608]{2,1,0:T(8,128)} fusion(f32[4,512,4608]{2,1,0:T(8,128)} %get-tuple-element.342, pred[]{:T(512)S(6)} %compare.4, bf16[4,64,512]{2,1,0:T(8,128)(2,1)S(1)} %copy-done.1, bf16[4,64,4608]{2,1,0:T(8,128)(2,1)S(1)} %reshape.108), kind=kOutput, calls=%fused_computation.clone.1 | convolution fusion | flops 1226833920 | bytes 78118912 | tf_op jit(solution)/shard_map/while/body/eval_jaxpr/bkx,bky->bxy/dot_general | solution.py:86
  429.6 3.7 copy.54
  433.3 2.2 copy.60
  435.6 54.3 %reshape.94 = f32[4,8,64,72,64]{4,3,2,1,0:T(8,128)} reshape(f32[4,512,4608]{2,1,0:T(8,128)} %get-tuple-element.183) | data formatting | bytes 75497472 | tf_op jit(solution)/shard_map/reshape | solution.py:98
  489.9 27.4 %fusion = f32[4,64,64,64]{3,2,1,0:T(8,128)} fusion(f32[4,8,64,72,64]{4,3,2,1,0:T(8,128)} %reshape.94), kind=kLoop, calls=%fused_computation.24 | loop fusion | flops 7340032 | bytes 37748736 | tf_op jit(solution)/shard_map/add | solution.py:103
  517.3 11.9 %rev.4 = f32[4,64,64,64]{3,2,1,0:T(8,128)} reverse(f32[4,64,64,64]{3,2,1,0:T(8,128)} %fusion), dimensions={2} | reverse | bytes 8388608 | tf_op jit(solution)/shard_map/jit(_flip)/rev | solution.py:104
  529.1 11.5 %copy.55 = f32[4,64,64,64]{3,2,1,0:T(8,128)} copy(f32[4,64,64,64]{3,1,2,0:T(8,128)} %bitcast.113) | data formatting | bytes 8388608 | tf_op jit(solution)/shard_map/transpose | solution.py:104
  540.6 7.9 %reshape.95 = f32[4,64,4096]{2,1,0:T(8,128)} reshape(f32[4,64,64,64]{3,2,1,0:T(8,128)} %copy.55) | data formatting | bytes 8388608 | tf_op jit(solution)/shard_map/reshape | solution.py:113
  549.9 154.3 %all-reduce.3.cloned.1.call-done = f32[4,64,4096]{2,1,0:T(8,128)} async-done(((f32[4,64,4096]{2,1,0:T(8,128)}), f32[4,64,4096]{2,1,0:T(8,128)}) %all-reduce.3.cloned.1.call-update) | async-done | bytes 4194320 | tf_op jit(solution)/shard_map/psum | solution.py:114
  704.2 2.1 multiply_reduce_fusion
  707.3 31.9 %psum.15 = f32[]{:T(128)} all-reduce(f32[]{:T(128)} %multiply_reduce_fusion), channel_id=1, replica_groups=mesh['case'=2,'tm'=4,'bundle'=2,'sub'=2] {'tm','bundle','sub'}, use_global_device_ids=true, to_apply=%region_5.6 | all-reduce | flops 1 | bytes 8 | tf_op jit(solution)/shard_map/psum | solution.py:118
  739.9 2.3 dynamic-slice_multiply_fusion
  (137 shorter events, 90.5 us)
Async XLA Ops:
  8.0 6.5 copy-start.2
  8.0 540.5 %reduce-scatter.2.cloned.1.call-start = ((), (), s32[]{:S(2)}) async-start(), calls=%async_computation.1 | async-start | bytes 3145728 | tf_op jit(solution)/shard_map/reduce_scatter | solution.py:105
  12.5 143.7 %collective-permute-start.1 = (bf16[128,4,64]{0,2,1:T(8,128)(2,1)S(1)}, bf16[128,4,64]{0,2,1:T(8,128)(2,1)S(1)}, u32[]{:S(2)}, u32[]{:S(2)}) collective-permute-start(bf16[128,4,64]{0,2,1:T(8,128)(2,1)S(1)} %slice.269), channel_id=1, source_target_pairs={{4,0},{8,4},{12,8},{5,1},{9,5},{13,9},{6,2},{10,6},{14,10},{7,3},{... | collective-permute-start | bytes 196616 | tf_op jit(solution)/shard_map/ppermute | solution.py:17
  15.3 143.3 %collective-permute-start = (bf16[128,4,64]{0,2,1:T(8,128)(2,1)S(1)}, bf16[128,4,64]{0,2,1:T(8,128)(2,1)S(1)}, u32[]{:S(2)}, u32[]{:S(2)}) collective-permute-start(bf16[128,4,64]{0,2,1:T(8,128)(2,1)S(1)} %slice.268), channel_id=1, source_target_pairs={{0,4},{4,8},{8,12},{1,5},{5,9},{9,13},{2,6},{6,10},{10,14},{3,7},{... | collective-permute-start | bytes 196616 | tf_op jit(solution)/shard_map/ppermute | solution.py:17
  25.6 7.2 copy-start
  195.2 7.9 %copy-start.1 = (bf16[4,64,512]{2,1,0:T(8,128)(2,1)S(1)}, bf16[4,64,512]{2,1,0:T(8,128)(2,1)}, u32[]{:S(2)}) copy-start(bf16[4,64,512]{2,1,0:T(8,128)(2,1)} %reshape.107) | copy-start | bytes 786436 | tf_op jit(solution)/shard_map/while
  252.6 7.9 %copy-start.1 = (bf16[4,64,512]{2,1,0:T(8,128)(2,1)S(1)}, bf16[4,64,512]{2,1,0:T(8,128)(2,1)}, u32[]{:S(2)}) copy-start(bf16[4,64,512]{2,1,0:T(8,128)(2,1)} %reshape.107) | copy-start | bytes 786436 | tf_op jit(solution)/shard_map/while
  323.4 7.9 %copy-start.1 = (bf16[4,64,512]{2,1,0:T(8,128)(2,1)S(1)}, bf16[4,64,512]{2,1,0:T(8,128)(2,1)}, u32[]{:S(2)}) copy-start(bf16[4,64,512]{2,1,0:T(8,128)(2,1)} %reshape.107) | copy-start | bytes 786436 | tf_op jit(solution)/shard_map/while
  394.2 7.9 %copy-start.1 = (bf16[4,64,512]{2,1,0:T(8,128)(2,1)S(1)}, bf16[4,64,512]{2,1,0:T(8,128)(2,1)}, u32[]{:S(2)}) copy-start(bf16[4,64,512]{2,1,0:T(8,128)(2,1)} %reshape.107) | copy-start | bytes 786436 | tf_op jit(solution)/shard_map/while
  435.5 268.7 %all-reduce.3.cloned.1.call-start = ((), (), s32[]{:S(2)}) async-start(), calls=%async_computation.2 | async-start | bytes 8388608 | tf_op jit(solution)/shard_map/psum | solution.py:114
Sparse Core Ops, SparseCore 0:
  435.7 10.2 reduce-scatter.1
Sparse Core Ops, SparseCore 1:
  548.6 155.6 all-reduce.2
where the time goes:
time: 755 us; the launch traced here: 750 us
  local copies, waits for them, and re-layouts  365 us (48%)
  waiting for transfers between devices  154 us (20%)
  matrix products  131 us (17%)
  other arithmetic  40.7 us (5%)
  blocking collectives  31.9 us (4%)
  between operations  17 us (2%)
    psum x1, waiting for transfers between devices, local(): grad_sum = lax.psum(grad_flat, 'tm')  154 us
    dot_general x4, matrix products, advance(): jnp.einsum('bkx,bky->bxy', row_block, earlier, preferred_element_type=jnp...  96.3 us
    while x72, local copies, waits for them, and re-layouts  56.9 us
    reshape x1, local copies, waits for them, and re-layouts, local(): grad_total.reshape(local_bundles, tile_rows, bundle_width, lag_count + ti...  54.3 us
    another operation x2, local copies, waits for them, and re-layouts, local(): jnp.stack([kernel_pad[:, tile_rows - shift_row:tile_rows - shift_row + la...  50.8 us
    reshape x8, local copies, waits for them, and re-layouts, tiles_of(): return wide.reshape(bundles, tile_count, (lag_count + tile_rows) * width)  49.2 us
    reshape x1, local copies, waits for them, and re-layouts, local(): toeplitz.reshape(local_bundles, (lag_count + tile_rows) * bundle_width, t...  49.1 us
    unnamed x16, local copies, waits for them, and re-layouts  35.8 us
  transfers between devices with their start and end apart: 4, of which 1 were waited for; matrix products, arithmetic and copies ran while one was open for 34% of the time, Pallas kernels for 0%

commit v1 on v0

--- a/solution.py
+++ b/solution.py
@@ -111,7 +111,10 @@
         jnp.bfloat16
     )
     grad_flat = grad_blocks.reshape(local_bundles, lag_count, bundle_width * bundle_width)
-    grad_sum = lax.psum(grad_flat, "tm")
+    size, grad_sum = (lax.axis_size("tm"), grad_flat)
+    for stride in [1 << k for k in range(size.bit_length() - 1)]:
+        swap = [(i_2, i_2 ^ stride) for i_2 in range(size)]
+        grad_sum = grad_sum + lax.ppermute(grad_sum, "tm", swap)
     share_cols = grad_flat.shape[2] // lax.axis_size("tm")
     own_grad = lax.dynamic_slice_in_dim(grad_sum, lax.axis_index("tm") * share_cols, share_cols, 2)
     own_squares = jnp.sum(own_grad * own_grad)

time: 755 us -> 874 us (1.16)
  waiting for transfers between devices: 154 us -> 263 us
    ppermute x0 -> x2, waiting for transfers between devices: none -> 263 us  [local(): grad_sum = grad_sum + lax.ppermute(grad_sum, 'tm', swap)]
    psum x1 -> x0, waiting for transfers between devices: 154 us -> none  [local(): grad_sum = lax.psum(grad_flat, 'tm')]
  transfers between devices with their start and end apart: 4 -> 5, of which waited for: 1 -> 2; matrix products, arithmetic and copies ran while one was open for 34% -> 17% of each run, Pallas kernels for 0% -> 0%
where the time goes in v1:
time: 874 us; the launch traced here: 868 us
  local copies, waits for them, and re-layouts  365 us (42%)
  waiting for transfers between devices  263 us (30%)
  matrix products  131 us (15%)
  other arithmetic  47.5 us (5%)
  blocking collectives  32.2 us (4%)
  between operations  15.5 us (2%)
  starting transfers between devices  11.7 us (1%)
    ppermute x2, waiting for transfers between devices, local(): grad_sum = grad_sum + lax.ppermute(grad_sum, 'tm', swap)  263 us
    dot_general x4, matrix products, advance(): jnp.einsum('bkx,bky->bxy', row_block, earlier, preferred_element_type=jnp...  96.4 us
    while x72, local copies, waits for them, and re-layouts  56.2 us
    reshape x1, local copies, waits for them, and re-layouts, local(): grad_total.reshape(local_bundles, tile_rows, bundle_width, lag_count + ti...  54 us
    another operation x2, local copies, waits for them, and re-layouts, local(): jnp.stack([kernel_pad[:, tile_rows - shift_row:tile_rows - shift_row + la...  50.7 us
    reshape x8, local copies, waits for them, and re-layouts, tiles_of(): return wide.reshape(bundles, tile_count, (lag_count + tile_rows) * width)  49.2 us
    reshape x1, local copies, waits for them, and re-layouts, local(): toeplitz.reshape(local_bundles, (lag_count + tile_rows) * bundle_width, t...  49.1 us
    unnamed x16, local copies, waits for them, and re-layouts  36 us
  transfers between devices with their start and end apart: 5, of which 2 were waited for; matrix products, arithmetic and copies ran while one was open for 17% of the time, Pallas kernels for 0%

profile of v1, /device:TPU:0, one launch (start us, length us, event | category | flops | bytes accessed | tf_op | source)
XLA Modules:
  0.0 868.1 jit_solution(16481597088719214614)
XLA Ops:
  7.2 1.6 copy.41
  8.8 2.1 convolution_convert_fusion
  14.4 5.6 collective-permute-start
  20.0 4.8 copy.43
  24.8 6.1 bitcast_dynamic-update-slice_fusion
  32.0 4.1 pad_maximum_fusion
  36.1 3.2 fusion.7
  39.3 3.2 fusion.6
  42.5 3.2 fusion.5
  45.8 3.3 fusion.4
  49.1 3.4 fusion.3
  52.4 3.3 fusion.2
  55.7 3.2 fusion.1
  58.9 47.4 %copy.50 = bf16[4,72,64,8,64]{4,3,2,1,0:T(8,128)(2,1)} copy(bf16[4,72,64,8,64]{1,4,3,2,0:T(8,128)(2,1)} %fusion.1) | data formatting | bytes 37748736 | tf_op jit(solution)/shard_map/stack | solution.py:59
  106.4 49.1 %reshape.92 = bf16[4,4608,512]{2,1,0:T(8,128)(2,1)} reshape(bf16[4,72,64,8,64]{4,3,2,1,0:T(8,128)(2,1)} %copy.50) | data formatting | bytes 37748736 | tf_op jit(solution)/shard_map/reshape | solution.py:66
  155.5 2.3 maximum_bitcast_fusion.1
  158.9 269.9 %while.17 = (s32[]{:T(128)}, f32[4,512,4608]{2,1,0:T(8,128)}, f32[4,4,512,64]{3,2,1,0:T(8,128)}, s32[4]{0:T(128)S(1)}, bf16[4,2048,64]{1,2,0:T(8,128)(2,1)}, /*i...) while((s32[]{:T(128)}, f32[4,512,4608]{2,1,0:T(8,128)}, ...), condition=%wide.region_1.2_spmd.clone, body=%wide.region_0.1_spmd.clone.sunk | while | flops 2434793472 | bytes 131072384 | solution.py:92
  172.6 6.1 reshape.109
  178.7 8.1 fusion.24
  196.1 6.1 reshape.108
  202.3 14.0 %select_add_fusion.2 = f32[4,512,4608]{2,1,0:T(8,128)} fusion(f32[4,512,4608]{2,1,0:T(8,128)} %get-tuple-element.342, pred[]{:T(512)S(6)} %compare.4, bf16[4,64,512]{2,1,0:T(8,128)(2,1)S(1)} %copy-done.1, bf16[4,64,4608]{2,1,0:T(8,128)(2,1)S(1)} %reshape.108), kind=kOutput, calls=%fused_computation.clone.1 | convolution fusion | flops 1226833920 | bytes 78118912 | tf_op jit(solution)/shard_map/while/body/eval_jaxpr/bkx,bky->bxy/dot_general | solution.py:86
  229.9 6.1 reshape.109
  236.0 8.1 fusion.24
  253.5 6.1 reshape.108
  259.6 27.5 %select_add_fusion.2 = f32[4,512,4608]{2,1,0:T(8,128)} fusion(f32[4,512,4608]{2,1,0:T(8,128)} %get-tuple-element.342, pred[]{:T(512)S(6)} %compare.4, bf16[4,64,512]{2,1,0:T(8,128)(2,1)S(1)} %copy-done.1, bf16[4,64,4608]{2,1,0:T(8,128)(2,1)S(1)} %reshape.108), kind=kOutput, calls=%fused_computation.clone.1 | convolution fusion | flops 1226833920 | bytes 78118912 | tf_op jit(solution)/shard_map/while/body/eval_jaxpr/bkx,bky->bxy/dot_general | solution.py:86
  300.8 6.1 reshape.109
  306.9 8.1 fusion.24
  324.3 6.1 reshape.108
  330.5 27.5 %select_add_fusion.2 = f32[4,512,4608]{2,1,0:T(8,128)} fusion(f32[4,512,4608]{2,1,0:T(8,128)} %get-tuple-element.342, pred[]{:T(512)S(6)} %compare.4, bf16[4,64,512]{2,1,0:T(8,128)(2,1)S(1)} %copy-done.1, bf16[4,64,4608]{2,1,0:T(8,128)(2,1)S(1)} %reshape.108), kind=kOutput, calls=%fused_computation.clone.1 | convolution fusion | flops 1226833920 | bytes 78118912 | tf_op jit(solution)/shard_map/while/body/eval_jaxpr/bkx,bky->bxy/dot_general | solution.py:86
  371.6 6.1 reshape.109
  377.7 8.1 fusion.24
  395.1 6.1 reshape.108
  401.3 27.5 %select_add_fusion.2 = f32[4,512,4608]{2,1,0:T(8,128)} fusion(f32[4,512,4608]{2,1,0:T(8,128)} %get-tuple-element.342, pred[]{:T(512)S(6)} %compare.4, bf16[4,64,512]{2,1,0:T(8,128)(2,1)S(1)} %copy-done.1, bf16[4,64,4608]{2,1,0:T(8,128)(2,1)S(1)} %reshape.108), kind=kOutput, calls=%fused_computation.clone.1 | convolution fusion | flops 1226833920 | bytes 78118912 | tf_op jit(solution)/shard_map/while/body/eval_jaxpr/bkx,bky->bxy/dot_general | solution.py:86
  428.8 54.0 %reshape.94 = f32[4,8,64,72,64]{4,3,2,1,0:T(8,128)} reshape(f32[4,512,4608]{2,1,0:T(8,128)} %get-tuple-element.183) | data formatting | bytes 75497472 | tf_op jit(solution)/shard_map/reshape | solution.py:98
  482.8 27.4 %fusion = f32[4,64,64,64]{3,2,1,0:T(8,128)} fusion(f32[4,8,64,72,64]{4,3,2,1,0:T(8,128)} %reshape.94), kind=kLoop, calls=%fused_computation.24 | loop fusion | flops 7340032 | bytes 37748736 | tf_op jit(solution)/shard_map/add | solution.py:103
  510.2 11.9 %rev.4 = f32[4,64,64,64]{3,2,1,0:T(8,128)} reverse(f32[4,64,64,64]{3,2,1,0:T(8,128)} %fusion), dimensions={2} | reverse | bytes 8388608 | tf_op jit(solution)/shard_map/jit(_flip)/rev | solution.py:104
  522.1 11.5 %copy.55 = f32[4,64,64,64]{3,2,1,0:T(8,128)} copy(f32[4,64,64,64]{3,1,2,0:T(8,128)} %bitcast.113) | data formatting | bytes 8388608 | tf_op jit(solution)/shard_map/transpose | solution.py:104
  533.6 7.9 reshape.95
  541.5 2.0 collective-permute-start.2
  543.5 3.7 copy.54
  547.2 2.2 copy.60
  549.5 84.4 %collective-permute-done.2 = f32[4,64,4096]{2,1,0:T(8,128)} collective-permute-done((f32[4,64,4096]{2,1,0:T(8,128)}, f32[4,64,4096]{2,1,0:T(8,128)}, u32[]{:S(2)}, u32[]{:S(2)}) %collective-permute-start.2) | collective-permute-done | bytes 4194336 | tf_op jit(solution)/shard_map/ppermute | solution.py:117
  633.8 6.1 add.155
  639.9 2.8 collective-permute-start.3
  644.0 178.2 %collective-permute-done.3 = f32[4,64,4096]{2,1,0:T(8,128)} collective-permute-done((f32[4,64,4096]{2,1,0:T(8,128)}, f32[4,64,4096]{2,1,0:T(8,128)}, u32[]{:S(2)}, u32[]{:S(2)}) %collective-permute-start.3) | collective-permute-done | bytes 4194336 | tf_op jit(solution)/shard_map/ppermute | solution.py:117
  822.1 2.4 multiply_reduce_fusion
  825.6 32.2 %psum.7 = f32[]{:T(128)} all-reduce(f32[]{:T(128)} %multiply_reduce_fusion), channel_id=1, replica_groups=mesh['case'=2,'tm'=4,'bundle'=2,'sub'=2] {'tm','bundle','sub'}, use_global_device_ids=true, to_apply=%region_4.5 | all-reduce | flops 1 | bytes 8 | tf_op jit(solution)/shard_map/psum | solution.py:121
  858.5 2.7 broadcast_multiply_fusion
  (139 shorter events, 96.2 us)
Async XLA Ops:
  7.2 6.5 copy-start.2
  7.2 635.5 %reduce-scatter.2.cloned.1.call-start = ((), (), s32[]{:S(2)}) async-start(), calls=%async_computation.1 | async-start | bytes 3145728 | tf_op jit(solution)/shard_map/reduce_scatter | solution.py:105
  11.7 143.8 %collective-permute-start.1 = (bf16[128,4,64]{0,2,1:T(8,128)(2,1)S(1)}, bf16[128,4,64]{0,2,1:T(8,128)(2,1)S(1)}, u32[]{:S(2)}, u32[]{:S(2)}) collective-permute-start(bf16[128,4,64]{0,2,1:T(8,128)(2,1)S(1)} %slice.269), channel_id=1, source_target_pairs={{4,0},{8,4},{12,8},{5,1},{9,5},{13,9},{6,2},{10,6},{14,10},{7,3},{... | collective-permute-start | bytes 196616 | tf_op jit(solution)/shard_map/ppermute | solution.py:17
  14.4 143.4 %collective-permute-start = (bf16[128,4,64]{0,2,1:T(8,128)(2,1)S(1)}, bf16[128,4,64]{0,2,1:T(8,128)(2,1)S(1)}, u32[]{:S(2)}, u32[]{:S(2)}) collective-permute-start(bf16[128,4,64]{0,2,1:T(8,128)(2,1)S(1)} %slice.268), channel_id=1, source_target_pairs={{0,4},{4,8},{8,12},{1,5},{5,9},{9,13},{2,6},{6,10},{10,14},{3,7},{... | collective-permute-start | bytes 196616 | tf_op jit(solution)/shard_map/ppermute | solution.py:17
  24.8 7.2 copy-start
  194.2 8.0 copy-start.1
  251.6 8.0 copy-start.1
  322.5 8.0 copy-start.1
  393.3 8.0 copy-start.1
  541.5 92.3 %collective-permute-start.2 = (f32[4,64,4096]{2,1,0:T(8,128)}, f32[4,64,4096]{2,1,0:T(8,128)}, u32[]{:S(2)}, u32[]{:S(2)}) collective-permute-start(f32[4,64,4096]{2,1,0:T(8,128)} %reshape.95), channel_id=1, source_target_pairs={{0,4},{4,0},{8,12},{12,8},{1,5},{5,1},{9,13},{13,9},{2,6},{6,2},{1... | collective-permute-start | bytes 12582920 | tf_op jit(solution)/shard_map/ppermute | solution.py:117
  639.9 182.3 %collective-permute-start.3 = (f32[4,64,4096]{2,1,0:T(8,128)}, f32[4,64,4096]{2,1,0:T(8,128)}, u32[]{:S(2)}, u32[]{:S(2)}) collective-permute-start(f32[4,64,4096]{2,1,0:T(8,128)} %add.155), channel_id=1, source_target_pairs={{0,8},{4,12},{8,0},{12,4},{1,9},{5,13},{9,1},{13,5},{2,10},{6,14},... | collective-permute-start | bytes 12582920 | tf_op jit(solution)/shard_map/ppermute | solution.py:117
Sparse Core Ops, SparseCore 0:
  549.6 9.7 reduce-scatter.1
